TPU v7x, 512 devices: a whole 4x4x16 slice. The times are simulated.
512 devices in a mesh: gx: 32 (over z_hi, x, core), gy: 4 (over y), gz: 4 (over z_lo).
Axes of the slice: x: 4, y: 4, z: 16 (z_hi: 4, z_lo: 4; z = z_hi * 4 + z_lo), core: 2. Of those that a mesh axis runs over, the one named last changes fastest.
Arguments:
- level_set: float32 [1024, 128, 512], P('gx', 'gy', 'gz'), may hold values from -6 to 6
- velocity: bfloat16 [3, 1024, 128, 512], P(None, 'gx', 'gy', 'gz'), may hold values from -1 to 1
- active_brick: int32 [32, 4, 4], P('gx', 'gy', 'gz'), may hold values 0 or 1
- depth_order: int32 [4], replicated, may hold values from 0 to 3, as said below
Outputs:
- level_out: float32 [1024, 128, 512], P('gx', 'gy', 'gz')
- image: float32 [4, 2048, 256], P(None, ('gx', 'gz'), 'gy')
Inputs may be any that keep to these rules, and one draw needn't show every extreme that they name: `depth_order`: either 0, 1, .. in slab order or the reverse.
All inputs are finite; a program needn't handle non-finite values. No bound on the sum of `active_brick` on one device may be relied on, other than what follows from the above.
Results may differ from a plain program's by a relative error of at most 0.0003.
Values may be sent and summed in bfloat16 or wider, within the bound.
No kernel may reach another device: no remote copies, remote signals or barrier semaphores. Data moves between devices by JAX's collectives and lax.ppermute only.
A program may use at most 64 MiB of HBM per device.

v0:
```python
import jax
import jax.numpy as jnp
from jax import lax
from jax.sharding import PartitionSpec as P

CZ = 128
time_step = 0.4
weno_floor = 1e-06


def extended(x, sides, width):
    for axis, dim in sides:
        size, length = (lax.axis_size(axis), x.shape[dim])
        up = [(i, (i + 1) % size) for i in range(size)]
        down = [(j, i) for i, j in up]
        last = lax.slice_in_dim(x, length - width, length, axis=dim)
        initial = lax.slice_in_dim(x, 0, width, axis=dim)
        before = lax.ppermute(last, axis, up)
        after = lax.ppermute(initial, axis, down)
        x = jnp.concatenate([before, x, after], axis=dim)
    return x


def square(operand):
    return operand * operand


def weno_value(diff_one, diff_two, diff_three, diff_four, diff_five):
    candidate_one = diff_one / 3.0 - 7.0 * diff_two / 6.0 + 11.0 * diff_three / 6.0
    candidate_two = -diff_two / 6.0 + 5.0 * diff_three / 6.0 + diff_four / 3.0
    candidate_three = diff_three / 3.0 + 5.0 * diff_four / 6.0 - diff_five / 6.0
    smooth_one = 13.0 / 12.0 * square(diff_one - 2.0 * diff_two + diff_three) + 0.25 * square(
        diff_one - 4.0 * diff_two + 3.0 * diff_three
    )
    smooth_two = 13.0 / 12.0 * square(diff_two - 2.0 * diff_three + diff_four) + 0.25 * square(
        diff_two - diff_four
    )
    smooth_three = 13.0 / 12.0 * square(diff_three - 2.0 * diff_four + diff_five) + 0.25 * square(
        3.0 * diff_three - 4.0 * diff_four + diff_five
    )
    weight_one = 0.1 / square(weno_floor + smooth_one)
    weight_two = 0.6 / square(weno_floor + smooth_two)
    weight_three = 0.3 / square(weno_floor + smooth_three)
    return (
        weight_one * candidate_one + weight_two * candidate_two + weight_three * candidate_three
    ) / (weight_one + weight_two + weight_three)


def window(padded, axis_dim, offset):
    slicing = [slice(3, extent - 3) for extent in padded.shape]
    length = padded.shape[axis_dim] - 6
    slicing[axis_dim] = slice(3 + offset, 3 + offset + length)
    return padded[tuple(slicing)]


def local_rate(padded, velocity_window):
    summed = jnp.zeros(velocity_window.shape[1:], jnp.float32)
    for axis_dim in range(3):
        jump_list = [
            window(padded, axis_dim, offset) - window(padded, axis_dim, offset - 1)
            for offset in range(-2, 4)
        ]
        from_left = weno_value(jump_list[0], jump_list[1], jump_list[2], jump_list[3], jump_list[4])
        from_right = weno_value(
            jump_list[5], jump_list[4], jump_list[3], jump_list[2], jump_list[1]
        )
        speed_axis = velocity_window[axis_dim].astype(jnp.float32)
        summed = (
            summed
            + jnp.maximum(speed_axis, 0.0) * from_left
            + jnp.minimum(speed_axis, 0.0) * from_right
        )
    return -summed


def shade(samples, alive, ascending):
    opacity = alive * (2.0 / CZ) / (1.0 + 4.0 * samples * samples)
    log_clear = jnp.log1p(-opacity)
    depth = jnp.arange(CZ)
    ahead = jnp.where(
        ascending, depth[:, None] < depth[None, :], depth[:, None] > depth[None, :]
    ).astype(jnp.float32)
    flat_logs = log_clear.reshape(-1, CZ)
    before = jnp.dot(flat_logs, ahead, precision=lax.Precision.HIGHEST).reshape(log_clear.shape)
    weight = jnp.exp(before) * opacity
    bright = jnp.tanh(samples)
    red = jnp.sum(weight * (0.5 + 0.5 * bright), -1)
    green = jnp.sum(weight * (0.5 - 0.5 * bright), -1)
    blue = jnp.sum(weight / (1.0 + samples * samples), -1)
    clear = jnp.exp(jnp.sum(log_clear, -1))
    return jnp.stack([red, green, blue, clear])


def alternate(grid_pairs):
    row_list = [jnp.stack(pixel_pair, -1) for pixel_pair in grid_pairs]
    joined = jnp.stack(row_list, -3)
    joined_shape = joined.shape
    return joined.reshape(joined_shape[:-4] + (joined_shape[-4] * 2, joined_shape[-2] * 2))


def over(front_part, back_part):
    colour = front_part[:3] + front_part[3:] * back_part[:3]
    clear = front_part[3:] * back_part[3:]
    return jnp.concatenate([colour, clear], 0)


def shards(level_set, velocity, active_brick, depth_order):

    def section_rate(level_field):
        padded = extended(level_field, (("gx", 0), ("gy", 1), ("gz", 2)), 3)
        return local_rate(padded, velocity)

    section_one = level_set + time_step * section_rate(level_set)
    section_two = 0.75 * level_set + 0.25 * (section_one + time_step * section_rate(section_one))
    advanced = level_set / 3.0 + 2.0 / 3.0 * (section_two + time_step * section_rate(section_two))
    alive = active_brick[0, 0, 0] > 0
    level_out = jnp.where(alive, advanced, level_set)
    alive_float = alive.astype(jnp.float32)
    group = lax.axis_size("gz")
    ascending = depth_order[0] < depth_order[group - 1]
    rim = extended(level_out.astype(jnp.bfloat16), (("gx", 0), ("gy", 1)), 1).astype(
        level_out.dtype
    )
    left_x = 0.75 * rim[1:-1] + 0.25 * rim[:-2]
    right_x = 0.75 * rim[1:-1] + 0.25 * rim[2:]
    grid_pairs = []
    for along_x in (left_x, right_x):
        pair_list = []
        for neighbour in (along_x[:, :-2], along_x[:, 2:]):
            samples = 0.75 * along_x[:, 1:-1] + 0.25 * neighbour
            pair_list.append(shade(samples, alive_float, ascending))
        grid_pairs.append(pair_list)
    slab_image = alternate(grid_pairs)
    rows_each = slab_image.shape[1] // group
    columns = slab_image.shape[2]
    pieces = slab_image.reshape(4, group, rows_each, columns)
    received = lax.all_to_all(pieces, "gz", split_axis=1, concat_axis=1, tiled=True)
    blended = jnp.concatenate(
        [
            jnp.zeros((3, rows_each, columns), jnp.float32),
            jnp.ones((1, rows_each, columns), jnp.float32),
        ],
        0,
    )
    for rank_value in range(group):
        chooser = (depth_order == rank_value).astype(jnp.float32)
        piece_now = jnp.einsum("s,csij->cij", chooser, received, precision=lax.Precision.HIGHEST)
        blended = over(blended, piece_now)
    image = jnp.concatenate([blended[:3], 1.0 - blended[3:]], 0)
    return (level_out, image)


def solution(mesh):
    placed = (P("gx", "gy", "gz"), P(None, "gx", "gy", "gz"), P("gx", "gy", "gz"), P())
    return jax.shard_map(
        shards,
        mesh=mesh,
        in_specs=placed,
        out_specs=(P("gx", "gy", "gz"), P(None, ("gx", "gz"), "gy")),
        check_vma=False,
    )
```

profile of v0, /device:TPU:32, one launch (start us, length us, event | category | flops | bytes accessed | tf_op | source)
XLA Modules:
  0.0 195.8 jit_solution(901559053685275974)
XLA Ops:
  3.4 13.5 %collective-permute-start.1 = (f32[3,32,128]{2,1,0:T(8,128)S(1)}, f32[3,32,128]{2,1,0:T(8,128)S(1)}, u32[]{:S(2)}, u32[]{:S(2)}) collective-permute-start(f32[3,32,128]{2,1,0:T(8,128)S(1)} %get-tuple-element.55), channel_id=1, source_target_pairs={{16,0},{32,16},{48,32},{64,48},{80,64},{96,80},{112,96},{128,112},... | collective-permute-start | bytes 147464 | tf_op jit(solution)/shard_map/ppermute | solution.py:19
  18.6 4.9 %collective-permute-start.3 = (f32[38,3,128]{2,1,0:T(4,128)S(1)}, f32[38,3,128]{2,1,0:T(4,128)S(1)}, u32[]{:S(2)}, u32[]{:S(2)}) collective-permute-start(f32[38,3,128]{2,1,0:T(4,128)S(1)} %get-tuple-element.47), channel_id=1, source_target_pairs={{4,0},{8,4},{12,8},{0,12},{5,1},{9,5},{13,9},{1,13},{6,2},{10,6},{... | collective-permute-start | bytes 175112 | tf_op jit(solution)/shard_map/ppermute | solution.py:19
  25.6 5.5 %collective-permute-done.2 = f32[38,3,128]{2,1,0:T(4,128)S(1)} collective-permute-done((f32[38,3,128]{2,1,0:T(4,128)S(1)}, f32[38,3,128]{2,1,0:T(4,128)S(1)}, u32[]{:S(2)}, u32[]{:S(2)}) %collective-permute-start.2) | collective-permute-done | bytes 58400 | tf_op jit(solution)/shard_map/ppermute | solution.py:18
  32.4 2.9 %collective-permute-start.4 = (f32[38,38,3]{1,0,2:T(8,128)}, f32[38,38,3]{1,0,2:T(8,128)S(1)}, u32[]{:S(2)}, u32[]{:S(2)}) collective-permute-start(f32[38,38,3]{1,0,2:T(8,128)} %copy.7), channel_id=1, source_target_pairs={{0,1},{1,2},{2,3},{3,0},{4,5},{5,6},{6,7},{7,4},{8,9},{9,10},{10,1... | collective-permute-start | bytes 51992 | tf_op jit(solution)/shard_map/ppermute | solution.py:18
  35.7 2.9 %collective-permute-start.5 = (f32[38,38,3]{1,0,2:T(8,128)S(1)}, f32[38,38,3]{1,0,2:T(8,128)S(1)}, u32[]{:S(2)}, u32[]{:S(2)}) collective-permute-start(f32[38,38,3]{1,0,2:T(8,128)S(1)} %copy.9), channel_id=1, source_target_pairs={{1,0},{2,1},{3,2},{0,3},{5,4},{6,5},{7,6},{4,7},{9,8},{10,9},{11,1... | collective-permute-start | bytes 51992 | tf_op jit(solution)/shard_map/ppermute | solution.py:19
  39.1 2.7 %collective-permute-done.5 = f32[38,38,3]{1,0,2:T(8,128)S(1)} collective-permute-done((f32[38,38,3]{1,0,2:T(8,128)S(1)}, f32[38,38,3]{1,0,2:T(8,128)S(1)}, u32[]{:S(2)}, u32[]{:S(2)}) %collective-permute-start.5) | collective-permute-done | bytes 17360 | tf_op jit(solution)/shard_map/ppermute | solution.py:19
  43.1 2.0 %maximum_maximum_fusion = (f32[38,38,131]{2,1,0:T(8,128)S(1)}, f32[38,38,131]{2,1,0:T(8,128)S(1)}) fusion(f32[38,3,128]{2,1,0:T(4,128)S(1)} %collective-permute-done.3, f32[38,32,128]{2,1,0:T(8,128)S(1)} %get-tuple-element.67, f32[38,3,128]{2,1,0:T(4,128)S(1)} %collective-permute-done.2, f32[38,38,3]{2,1,0:T(8,128)S(1)} %copy.8, f32[38,38,3]{2,1,0:T(8,128)} %copy.10), kind=kLoop, calls=%fused_computation | loop fusion | flops 1134984 | bytes 2287296 | tf_op jit(solution)/shard_map/concatenate | solution.py:20
  45.1 8.4 %fusion.27 = f32[32,32,128]{2,1,0:T(8,128)S(1)} fusion(f32[32,32,128]{2,1,0:T(8,128)S(1)} %copy-done, f32[38,38,131]{2,1,0:T(8,128)S(1)} %get-tuple-element.29, f32[38,38,131]{2,1,0:T(8,128)S(1)} %get-tuple-element.28, f32[38,3,128]{2,1,0:T(4,128)S(1)} %collective-permute-done.3, f32[38,32,128]{2,1,0:T(8,128)S(1)} %get-tuple-element.67, ...), kind=kLoop, calls=%fused_computation.81 | loop fusion | flops 54919168 | bytes 8865792 | tf_op jit(solution)/shard_map/add | solution.py:113
  53.5 7.0 %collective-permute-start.7 = (f32[3,32,128]{2,1,0:T(8,128)S(1)}, f32[3,32,128]{2,1,0:T(8,128)S(1)}, u32[]{:S(2)}, u32[]{:S(2)}) collective-permute-start(f32[3,32,128]{2,1,0:T(8,128)S(1)} %get-tuple-element.51), channel_id=1, source_target_pairs={{16,0},{32,16},{48,32},{64,48},{80,64},{96,80},{112,96},{128,112},... | collective-permute-start | bytes 147464 | tf_op jit(solution)/shard_map/ppermute | solution.py:19
  62.4 9.7 %collective-permute-done.6 = f32[3,32,128]{2,1,0:T(8,128)S(1)} collective-permute-done((f32[3,32,128]{2,1,0:T(8,128)S(1)}, f32[3,32,128]{2,1,0:T(8,128)S(1)}, u32[]{:S(2)}, u32[]{:S(2)}) %collective-permute-start.6) | collective-permute-done | bytes 49184 | tf_op jit(solution)/shard_map/ppermute | solution.py:18
  74.1 3.9 %collective-permute-start.8 = (f32[38,3,128]{2,1,0:T(4,128)S(1)}, f32[38,3,128]{2,1,0:T(4,128)S(1)}, u32[]{:S(2)}, u32[]{:S(2)}) collective-permute-start(f32[38,3,128]{2,1,0:T(4,128)S(1)} %get-tuple-element.44), channel_id=1, source_target_pairs={{0,4},{4,8},{8,12},{12,0},{1,5},{5,9},{9,13},{13,1},{2,6},{6,10},{... | collective-permute-start | bytes 175112 | tf_op jit(solution)/shard_map/ppermute | solution.py:18
  78.5 3.1 %collective-permute-done.8 = f32[38,3,128]{2,1,0:T(4,128)S(1)} collective-permute-done((f32[38,3,128]{2,1,0:T(4,128)S(1)}, f32[38,3,128]{2,1,0:T(4,128)S(1)}, u32[]{:S(2)}, u32[]{:S(2)}) %collective-permute-start.8) | collective-permute-done | bytes 58400 | tf_op jit(solution)/shard_map/ppermute | solution.py:18
  82.3 3.4 %collective-permute-start.10 = (f32[38,38,3]{1,0,2:T(8,128)S(1)}, f32[38,38,3]{1,0,2:T(8,128)S(1)}, u32[]{:S(2)}, u32[]{:S(2)}) collective-permute-start(f32[38,38,3]{1,0,2:T(8,128)S(1)} %copy.11), channel_id=1, source_target_pairs={{0,1},{1,2},{2,3},{3,0},{4,5},{5,6},{6,7},{7,4},{8,9},{9,10},{10,1... | collective-permute-start | bytes 51992 | tf_op jit(solution)/shard_map/ppermute | solution.py:18
  86.1 2.4 %collective-permute-start.11 = (f32[38,38,3]{1,0,2:T(8,128)S(1)}, f32[38,38,3]{1,0,2:T(8,128)S(1)}, u32[]{:S(2)}, u32[]{:S(2)}) collective-permute-start(f32[38,38,3]{1,0,2:T(8,128)S(1)} %copy.13), channel_id=1, source_target_pairs={{1,0},{2,1},{3,2},{0,3},{5,4},{6,5},{7,6},{4,7},{9,8},{10,9},{11,1... | collective-permute-start | bytes 51992 | tf_op jit(solution)/shard_map/ppermute | solution.py:19
  90.0 3.1 %collective-permute-done.11 = f32[38,38,3]{1,0,2:T(8,128)S(1)} collective-permute-done((f32[38,38,3]{1,0,2:T(8,128)S(1)}, f32[38,38,3]{1,0,2:T(8,128)S(1)}, u32[]{:S(2)}, u32[]{:S(2)}) %collective-permute-start.11) | collective-permute-done | bytes 17360 | tf_op jit(solution)/shard_map/ppermute | solution.py:19
  94.4 2.2 %maximum_maximum_fusion.1 = (f32[38,38,131]{2,1,0:T(8,128)S(1)}, f32[38,38,131]{2,1,0:T(8,128)S(1)}) fusion(f32[38,3,128]{2,1,0:T(4,128)S(1)} %collective-permute-done.9, f32[3,32,128]{2,1,0:T(8,128)S(1)} %collective-permute-done.7, f32[32,32,128]{2,1,0:T(8,128)S(1)} %fusion.27, f32[3,32,128]{2,1,0:T(8,128)S(1)} %collective-permute-done.6, ...), kind=kLoop, calls=%fused_computation.2 | loop fusion | flops 1891640 | bytes 2287296 | tf_op jit(solution)/shard_map/concatenate | solution.py:20
  96.6 8.6 %fusion.37 = f32[32,32,128]{2,1,0:T(8,128)S(1)} fusion(f32[32,32,128]{2,1,0:T(8,128)S(1)} %fusion.27, f32[38,38,131]{2,1,0:T(8,128)S(1)} %get-tuple-element.25, f32[38,38,131]{2,1,0:T(8,128)S(1)} %get-tuple-element.24, f32[38,35,128]{2,1,0:T(8,128)S(1)} %get-tuple-element.43, f32[38,35,128]{2,1,0:T(8,128)S(1)} %get-tuple-element.42, ...), kind=kLoop, calls=%fused_computation.91 | loop fusion | flops 55312384 | bytes 8749056 | tf_op jit(solution)/shard_map/add | solution.py:114
  105.2 1.9 collective-permute-start.13
  107.1 2.4 %collective-permute-start.12 = (f32[3,32,128]{2,1,0:T(8,128)S(1)}, f32[3,32,128]{2,1,0:T(8,128)S(1)}, u32[]{:S(2)}, u32[]{:S(2)}) collective-permute-start(f32[3,32,128]{2,1,0:T(8,128)S(1)} %get-tuple-element.48), channel_id=1, source_target_pairs={{0,16},{16,32},{32,48},{48,64},{64,80},{80,96},{96,112},{112,128},... | collective-permute-start | bytes 147464 | tf_op jit(solution)/shard_map/ppermute | solution.py:18
  109.5 9.6 %collective-permute-done.12 = f32[3,32,128]{2,1,0:T(8,128)S(1)} collective-permute-done((f32[3,32,128]{2,1,0:T(8,128)S(1)}, f32[3,32,128]{2,1,0:T(8,128)S(1)}, u32[]{:S(2)}, u32[]{:S(2)}) %collective-permute-start.12) | collective-permute-done | bytes 49184 | tf_op jit(solution)/shard_map/ppermute | solution.py:18
  121.1 3.9 %collective-permute-start.14 = (f32[38,3,128]{2,1,0:T(4,128)S(1)}, f32[38,3,128]{2,1,0:T(4,128)S(1)}, u32[]{:S(2)}, u32[]{:S(2)}) collective-permute-start(f32[38,3,128]{2,1,0:T(4,128)S(1)} %get-tuple-element.40), channel_id=1, source_target_pairs={{0,4},{4,8},{8,12},{12,0},{1,5},{5,9},{9,13},{13,1},{2,6},{6,10},{... | collective-permute-start | bytes 175112 | tf_op jit(solution)/shard_map/ppermute | solution.py:18
  125.7 2.9 %collective-permute-done.14 = f32[38,3,128]{2,1,0:T(4,128)S(1)} collective-permute-done((f32[38,3,128]{2,1,0:T(4,128)S(1)}, f32[38,3,128]{2,1,0:T(4,128)S(1)}, u32[]{:S(2)}, u32[]{:S(2)}) %collective-permute-start.14) | collective-permute-done | bytes 58400 | tf_op jit(solution)/shard_map/ppermute | solution.py:18
  129.3 3.9 %collective-permute-start.16 = (f32[38,38,3]{1,0,2:T(8,128)S(1)}, f32[38,38,3]{1,0,2:T(8,128)S(1)}, u32[]{:S(2)}, u32[]{:S(2)}) collective-permute-start(f32[38,38,3]{1,0,2:T(8,128)S(1)} %copy.15), channel_id=1, source_target_pairs={{0,1},{1,2},{2,3},{3,0},{4,5},{5,6},{6,7},{7,4},{8,9},{9,10},{10,1... | collective-permute-start | bytes 51992 | tf_op jit(solution)/shard_map/ppermute | solution.py:18
  133.6 2.1 %collective-permute-start.17 = (f32[38,38,3]{1,0,2:T(8,128)S(1)}, f32[38,38,3]{1,0,2:T(8,128)S(1)}, u32[]{:S(2)}, u32[]{:S(2)}) collective-permute-start(f32[38,38,3]{1,0,2:T(8,128)S(1)} %copy.17), channel_id=1, source_target_pairs={{1,0},{2,1},{3,2},{0,3},{5,4},{6,5},{7,6},{4,7},{9,8},{10,9},{11,1... | collective-permute-start | bytes 51992 | tf_op jit(solution)/shard_map/ppermute | solution.py:19
  137.1 2.6 %collective-permute-done.17 = f32[38,38,3]{1,0,2:T(8,128)S(1)} collective-permute-done((f32[38,38,3]{1,0,2:T(8,128)S(1)}, f32[38,38,3]{1,0,2:T(8,128)S(1)}, u32[]{:S(2)}, u32[]{:S(2)}) %collective-permute-start.17) | collective-permute-done | bytes 17360 | tf_op jit(solution)/shard_map/ppermute | solution.py:19
  141.0 2.2 %maximum_maximum_fusion.2 = (f32[38,38,131]{2,1,0:T(8,128)S(1)}, f32[38,38,131]{2,1,0:T(8,128)S(1)}) fusion(f32[38,3,128]{2,1,0:T(4,128)S(1)} %collective-permute-done.15, f32[3,32,128]{2,1,0:T(8,128)S(1)} %collective-permute-done.13, f32[32,32,128]{2,1,0:T(8,128)S(1)} %fusion.37, f32[3,32,128]{2,1,0:T(8,128)S(1)} %collective-permute-done.12, ...), kind=kLoop, calls=%fused_computation.4 | loop fusion | flops 1891640 | bytes 2287296 | tf_op jit(solution)/shard_map/concatenate | solution.py:20
  143.2 9.4 %fusion.219 = (bf16[32,32,128]{2,1,0:T(8,128)(2,1)S(1)}, f32[32,32,128]{2,1,0:T(8,128)}) fusion(f32[32,32,128]{2,1,0:T(8,128)S(1)} %copy-done, f32[32,32,128]{2,1,0:T(8,128)S(1)} %fusion.37, f32[38,38,131]{2,1,0:T(8,128)S(1)} %get-tuple-element.21, f32[38,38,131]{2,1,0:T(8,128)S(1)} %get-tuple-element.20, bf16[3,32,32,128]{3,2,1,0:T(8,128)(2,1)S(1)} %copy-done.3, ...), kind=kLoop, calls=%fused_computation.358 | loop fusion | flops 55574528 | bytes 9011201 | tf_op jit(solution)/shard_map/convert_element_type | solution.py:121
  154.5 2.4 %collective-permute-start.18 = (bf16[1,32,128]{2,1,0:T(8,128)(2,1)S(1)}, bf16[1,32,128]{2,1,0:T(8,128)(2,1)S(1)}, u32[]{:S(2)}, u32[]{:S(2)}) collective-permute-start(bf16[1,32,128]{2,1,0:T(8,128)(2,1)S(1)} %get-tuple-element.59), channel_id=1, source_target_pairs={{0,16},{16,32},{32,48},{48,64},{64,80},{80,96},{96,112},{112,128},... | collective-permute-start | bytes 24584 | tf_op jit(solution)/shard_map/ppermute | solution.py:18
  156.9 8.6 %collective-permute-done.18 = bf16[1,32,128]{2,1,0:T(8,128)(2,1)S(1)} collective-permute-done((bf16[1,32,128]{2,1,0:T(8,128)(2,1)S(1)}, bf16[1,32,128]{2,1,0:T(8,128)(2,1)S(1)}, u32[]{:S(2)}, u32[]{:S(2)}) %collective-permute-start.18) | collective-permute-done | bytes 8224 | tf_op jit(solution)/shard_map/ppermute | solution.py:18
  165.5 2.2 %collective-permute-start.21 = (bf16[34,1,128]{2,1,0:T(2,128)(2,1)S(1)}, bf16[34,1,128]{2,1,0:T(2,128)(2,1)S(1)}, u32[]{:S(2)}, u32[]{:S(2)}) collective-permute-start(bf16[34,1,128]{2,1,0:T(2,128)(2,1)S(1)} %get-tuple-element.58), channel_id=1, source_target_pairs={{4,0},{8,4},{12,8},{0,12},{5,1},{9,5},{13,9},{1,13},{6,2},{10,6},{... | collective-permute-start | bytes 26120 | tf_op jit(solution)/shard_map/ppermute | solution.py:19
  167.7 3.6 %collective-permute-start.20 = (bf16[34,1,128]{2,1,0:T(2,128)(2,1)S(1)}, bf16[34,1,128]{2,1,0:T(2,128)(2,1)S(1)}, u32[]{:S(2)}, u32[]{:S(2)}) collective-permute-start(bf16[34,1,128]{2,1,0:T(2,128)(2,1)S(1)} %get-tuple-element.57), channel_id=1, source_target_pairs={{0,4},{4,8},{8,12},{12,0},{1,5},{5,9},{9,13},{13,1},{2,6},{6,10},{... | collective-permute-start | bytes 26120 | tf_op jit(solution)/shard_map/ppermute | solution.py:18
  182.1 10.3 %all_to_all.5 = f32[4,1,4096]{2,1,0:T(1,128)S(1)} all-to-all(f32[4,1,4096]{2,1,0:T(1,128)S(1)} %reshape.79), channel_id=1, replica_groups=mesh['gx'=32,'gy'=4,'gz'=4] {'gz'}, dimensions={0} | all-to-all | bytes 131072 | tf_op jit(solution)/shard_map/all_to_all | solution.py:137
  (92 shorter events, 38.6 us)
Async XLA Ops:
  1.5 15.4 %collective-permute-start = (f32[3,32,128]{2,1,0:T(8,128)S(1)}, f32[3,32,128]{2,1,0:T(8,128)S(1)}, u32[]{:S(2)}, u32[]{:S(2)}) collective-permute-start(f32[3,32,128]{2,1,0:T(8,128)S(1)} %get-tuple-element.56), channel_id=1, source_target_pairs={{0,16},{16,32},{32,48},{48,64},{64,80},{80,96},{96,112},{112,128},... | collective-permute-start | bytes 147464 | tf_op jit(solution)/shard_map/ppermute | solution.py:18
  3.4 15.2 %collective-permute-start.1 = (f32[3,32,128]{2,1,0:T(8,128)S(1)}, f32[3,32,128]{2,1,0:T(8,128)S(1)}, u32[]{:S(2)}, u32[]{:S(2)}) collective-permute-start(f32[3,32,128]{2,1,0:T(8,128)S(1)} %get-tuple-element.55), channel_id=1, source_target_pairs={{16,0},{32,16},{48,32},{64,48},{80,64},{96,80},{112,96},{128,112},... | collective-permute-start | bytes 147464 | tf_op jit(solution)/shard_map/ppermute | solution.py:19
  18.6 6.9 %collective-permute-start.3 = (f32[38,3,128]{2,1,0:T(4,128)S(1)}, f32[38,3,128]{2,1,0:T(4,128)S(1)}, u32[]{:S(2)}, u32[]{:S(2)}) collective-permute-start(f32[38,3,128]{2,1,0:T(4,128)S(1)} %get-tuple-element.47), channel_id=1, source_target_pairs={{4,0},{8,4},{12,8},{0,12},{5,1},{9,5},{13,9},{1,13},{6,2},{10,6},{... | collective-permute-start | bytes 175112 | tf_op jit(solution)/shard_map/ppermute | solution.py:19
  23.6 7.5 %collective-permute-start.2 = (f32[38,3,128]{2,1,0:T(4,128)S(1)}, f32[38,3,128]{2,1,0:T(4,128)S(1)}, u32[]{:S(2)}, u32[]{:S(2)}) collective-permute-start(f32[38,3,128]{2,1,0:T(4,128)S(1)} %get-tuple-element.46), channel_id=1, source_target_pairs={{0,4},{4,8},{8,12},{12,0},{1,5},{5,9},{9,13},{13,1},{2,6},{6,10},{... | collective-permute-start | bytes 175112 | tf_op jit(solution)/shard_map/ppermute | solution.py:18
  32.4 6.3 %collective-permute-start.4 = (f32[38,38,3]{1,0,2:T(8,128)}, f32[38,38,3]{1,0,2:T(8,128)S(1)}, u32[]{:S(2)}, u32[]{:S(2)}) collective-permute-start(f32[38,38,3]{1,0,2:T(8,128)} %copy.7), channel_id=1, source_target_pairs={{0,1},{1,2},{2,3},{3,0},{4,5},{5,6},{6,7},{7,4},{8,9},{9,10},{10,1... | collective-permute-start | bytes 51992 | tf_op jit(solution)/shard_map/ppermute | solution.py:18
  35.7 6.1 %collective-permute-start.5 = (f32[38,38,3]{1,0,2:T(8,128)S(1)}, f32[38,38,3]{1,0,2:T(8,128)S(1)}, u32[]{:S(2)}, u32[]{:S(2)}) collective-permute-start(f32[38,38,3]{1,0,2:T(8,128)S(1)} %copy.9), channel_id=1, source_target_pairs={{1,0},{2,1},{3,2},{0,3},{5,4},{6,5},{7,6},{4,7},{9,8},{10,9},{11,1... | collective-permute-start | bytes 51992 | tf_op jit(solution)/shard_map/ppermute | solution.py:19
  43.1 2.0 %copy-start = (f32[32,32,128]{2,1,0:T(8,128)S(1)}, f32[32,32,128]{2,1,0:T(8,128)}, u32[]{:S(2)}) copy-start(f32[32,32,128]{2,1,0:T(8,128)} %param.4) | copy-start | bytes 1572868
  43.1 2.0 %copy-start.1 = (bf16[3,32,32,128]{3,2,1,0:T(8,128)(2,1)S(1)}, bf16[3,32,32,128]{3,2,1,0:T(8,128)(2,1)}, u32[]{:S(2)}) copy-start(bf16[3,32,32,128]{3,2,1,0:T(8,128)(2,1)} %param.5) | copy-start | bytes 2359300
  53.5 8.9 %collective-permute-start.7 = (f32[3,32,128]{2,1,0:T(8,128)S(1)}, f32[3,32,128]{2,1,0:T(8,128)S(1)}, u32[]{:S(2)}, u32[]{:S(2)}) collective-permute-start(f32[3,32,128]{2,1,0:T(8,128)S(1)} %get-tuple-element.51), channel_id=1, source_target_pairs={{16,0},{32,16},{48,32},{64,48},{80,64},{96,80},{112,96},{128,112},... | collective-permute-start | bytes 147464 | tf_op jit(solution)/shard_map/ppermute | solution.py:19
  60.5 11.6 %collective-permute-start.6 = (f32[3,32,128]{2,1,0:T(8,128)S(1)}, f32[3,32,128]{2,1,0:T(8,128)S(1)}, u32[]{:S(2)}, u32[]{:S(2)}) collective-permute-start(f32[3,32,128]{2,1,0:T(8,128)S(1)} %get-tuple-element.50), channel_id=1, source_target_pairs={{0,16},{16,32},{32,48},{48,64},{64,80},{80,96},{96,112},{112,128},... | collective-permute-start | bytes 147464 | tf_op jit(solution)/shard_map/ppermute | solution.py:18
  72.2 6.3 %collective-permute-start.9 = (f32[38,3,128]{2,1,0:T(4,128)S(1)}, f32[38,3,128]{2,1,0:T(4,128)S(1)}, u32[]{:S(2)}, u32[]{:S(2)}) collective-permute-start(f32[38,3,128]{2,1,0:T(4,128)S(1)} %get-tuple-element.45), channel_id=1, source_target_pairs={{4,0},{8,4},{12,8},{0,12},{5,1},{9,5},{13,9},{1,13},{6,2},{10,6},{... | collective-permute-start | bytes 175112 | tf_op jit(solution)/shard_map/ppermute | solution.py:19
  74.1 7.5 %collective-permute-start.8 = (f32[38,3,128]{2,1,0:T(4,128)S(1)}, f32[38,3,128]{2,1,0:T(4,128)S(1)}, u32[]{:S(2)}, u32[]{:S(2)}) collective-permute-start(f32[38,3,128]{2,1,0:T(4,128)S(1)} %get-tuple-element.44), channel_id=1, source_target_pairs={{0,4},{4,8},{8,12},{12,0},{1,5},{5,9},{9,13},{13,1},{2,6},{6,10},{... | collective-permute-start | bytes 175112 | tf_op jit(solution)/shard_map/ppermute | solution.py:18
  82.3 6.4 %collective-permute-start.10 = (f32[38,38,3]{1,0,2:T(8,128)S(1)}, f32[38,38,3]{1,0,2:T(8,128)S(1)}, u32[]{:S(2)}, u32[]{:S(2)}) collective-permute-start(f32[38,38,3]{1,0,2:T(8,128)S(1)} %copy.11), channel_id=1, source_target_pairs={{0,1},{1,2},{2,3},{3,0},{4,5},{5,6},{6,7},{7,4},{8,9},{9,10},{10,1... | collective-permute-start | bytes 51992 | tf_op jit(solution)/shard_map/ppermute | solution.py:18
  86.1 7.0 %collective-permute-start.11 = (f32[38,38,3]{1,0,2:T(8,128)S(1)}, f32[38,38,3]{1,0,2:T(8,128)S(1)}, u32[]{:S(2)}, u32[]{:S(2)}) collective-permute-start(f32[38,38,3]{1,0,2:T(8,128)S(1)} %copy.13), channel_id=1, source_target_pairs={{1,0},{2,1},{3,2},{0,3},{5,4},{6,5},{7,6},{4,7},{9,8},{10,9},{11,1... | collective-permute-start | bytes 51992 | tf_op jit(solution)/shard_map/ppermute | solution.py:19
  94.4 2.2 %copy-start.2 = (bf16[3,32,32,128]{3,2,1,0:T(8,128)(2,1)S(1)}, bf16[3,32,32,128]{3,2,1,0:T(8,128)(2,1)}, u32[]{:S(2)}) copy-start(bf16[3,32,32,128]{3,2,1,0:T(8,128)(2,1)} %param.5) | copy-start | bytes 2359300
  105.2 4.3 %collective-permute-start.13 = (f32[3,32,128]{2,1,0:T(8,128)S(1)}, f32[3,32,128]{2,1,0:T(8,128)S(1)}, u32[]{:S(2)}, u32[]{:S(2)}) collective-permute-start(f32[3,32,128]{2,1,0:T(8,128)S(1)} %get-tuple-element.49), channel_id=1, source_target_pairs={{16,0},{32,16},{48,32},{64,48},{80,64},{96,80},{112,96},{128,112},... | collective-permute-start | bytes 147464 | tf_op jit(solution)/shard_map/ppermute | solution.py:19
  107.1 12.0 %collective-permute-start.12 = (f32[3,32,128]{2,1,0:T(8,128)S(1)}, f32[3,32,128]{2,1,0:T(8,128)S(1)}, u32[]{:S(2)}, u32[]{:S(2)}) collective-permute-start(f32[3,32,128]{2,1,0:T(8,128)S(1)} %get-tuple-element.48), channel_id=1, source_target_pairs={{0,16},{16,32},{32,48},{48,64},{64,80},{80,96},{96,112},{112,128},... | collective-permute-start | bytes 147464 | tf_op jit(solution)/shard_map/ppermute | solution.py:18
  119.1 6.5 %collective-permute-start.15 = (f32[38,3,128]{2,1,0:T(4,128)S(1)}, f32[38,3,128]{2,1,0:T(4,128)S(1)}, u32[]{:S(2)}, u32[]{:S(2)}) collective-permute-start(f32[38,3,128]{2,1,0:T(4,128)S(1)} %get-tuple-element.41), channel_id=1, source_target_pairs={{4,0},{8,4},{12,8},{0,12},{5,1},{9,5},{13,9},{1,13},{6,2},{10,6},{... | collective-permute-start | bytes 175112 | tf_op jit(solution)/shard_map/ppermute | solution.py:19
  121.1 7.5 %collective-permute-start.14 = (f32[38,3,128]{2,1,0:T(4,128)S(1)}, f32[38,3,128]{2,1,0:T(4,128)S(1)}, u32[]{:S(2)}, u32[]{:S(2)}) collective-permute-start(f32[38,3,128]{2,1,0:T(4,128)S(1)} %get-tuple-element.40), channel_id=1, source_target_pairs={{0,4},{4,8},{8,12},{12,0},{1,5},{5,9},{9,13},{13,1},{2,6},{6,10},{... | collective-permute-start | bytes 175112 | tf_op jit(solution)/shard_map/ppermute | solution.py:18
  129.3 6.5 %collective-permute-start.16 = (f32[38,38,3]{1,0,2:T(8,128)S(1)}, f32[38,38,3]{1,0,2:T(8,128)S(1)}, u32[]{:S(2)}, u32[]{:S(2)}) collective-permute-start(f32[38,38,3]{1,0,2:T(8,128)S(1)} %copy.15), channel_id=1, source_target_pairs={{0,1},{1,2},{2,3},{3,0},{4,5},{5,6},{6,7},{7,4},{8,9},{9,10},{10,1... | collective-permute-start | bytes 51992 | tf_op jit(solution)/shard_map/ppermute | solution.py:18
  133.6 6.1 %collective-permute-start.17 = (f32[38,38,3]{1,0,2:T(8,128)S(1)}, f32[38,38,3]{1,0,2:T(8,128)S(1)}, u32[]{:S(2)}, u32[]{:S(2)}) collective-permute-start(f32[38,38,3]{1,0,2:T(8,128)S(1)} %copy.17), channel_id=1, source_target_pairs={{1,0},{2,1},{3,2},{0,3},{5,4},{6,5},{7,6},{4,7},{9,8},{10,9},{11,1... | collective-permute-start | bytes 51992 | tf_op jit(solution)/shard_map/ppermute | solution.py:19
  141.0 2.2 %copy-start.3 = (bf16[3,32,32,128]{3,2,1,0:T(8,128)(2,1)S(1)}, bf16[3,32,32,128]{3,2,1,0:T(8,128)(2,1)}, u32[]{:S(2)}) copy-start(bf16[3,32,32,128]{3,2,1,0:T(8,128)(2,1)} %param.5) | copy-start | bytes 2359300
  143.2 28.2 %copy-start.4 = (s32[4]{0:T(128)S(1)}, s32[4]{0:T(128)}, u32[]{:S(2)}) copy-start(s32[4]{0:T(128)} %param.7) | copy-start | bytes 52
  152.5 4.3 %collective-permute-start.19 = (bf16[1,32,128]{2,1,0:T(8,128)(2,1)S(1)}, bf16[1,32,128]{2,1,0:T(8,128)(2,1)S(1)}, u32[]{:S(2)}, u32[]{:S(2)}) collective-permute-start(bf16[1,32,128]{2,1,0:T(8,128)(2,1)S(1)} %get-tuple-element.60), channel_id=1, source_target_pairs={{16,0},{32,16},{48,32},{64,48},{80,64},{96,80},{112,96},{128,112},... | collective-permute-start | bytes 24584 | tf_op jit(solution)/shard_map/ppermute | solution.py:19
  154.5 11.0 %collective-permute-start.18 = (bf16[1,32,128]{2,1,0:T(8,128)(2,1)S(1)}, bf16[1,32,128]{2,1,0:T(8,128)(2,1)S(1)}, u32[]{:S(2)}, u32[]{:S(2)}) collective-permute-start(bf16[1,32,128]{2,1,0:T(8,128)(2,1)S(1)} %get-tuple-element.59), channel_id=1, source_target_pairs={{0,16},{16,32},{32,48},{48,64},{64,80},{80,96},{96,112},{112,128},... | collective-permute-start | bytes 24584 | tf_op jit(solution)/shard_map/ppermute | solution.py:18
  165.5 7.6 %collective-permute-start.21 = (bf16[34,1,128]{2,1,0:T(2,128)(2,1)S(1)}, bf16[34,1,128]{2,1,0:T(2,128)(2,1)S(1)}, u32[]{:S(2)}, u32[]{:S(2)}) collective-permute-start(bf16[34,1,128]{2,1,0:T(2,128)(2,1)S(1)} %get-tuple-element.58), channel_id=1, source_target_pairs={{4,0},{8,4},{12,8},{0,12},{5,1},{9,5},{13,9},{1,13},{6,2},{10,6},{... | collective-permute-start | bytes 26120 | tf_op jit(solution)/shard_map/ppermute | solution.py:19
  167.7 6.9 %collective-permute-start.20 = (bf16[34,1,128]{2,1,0:T(2,128)(2,1)S(1)}, bf16[34,1,128]{2,1,0:T(2,128)(2,1)S(1)}, u32[]{:S(2)}, u32[]{:S(2)}) collective-permute-start(bf16[34,1,128]{2,1,0:T(2,128)(2,1)S(1)} %get-tuple-element.57), channel_id=1, source_target_pairs={{0,4},{4,8},{8,12},{12,0},{1,5},{5,9},{9,13},{13,1},{2,6},{6,10},{... | collective-permute-start | bytes 26120 | tf_op jit(solution)/shard_map/ppermute | solution.py:18
where the time goes:
time: 197 us; the launch traced here: 196 us
  starting transfers between devices  75 us (38%)
  waiting for transfers between devices  50.3 us (26%)
  other arithmetic  35.4 us (18%)
  local copies, waits for them, and re-layouts  15.9 us (8%)
  blocking collectives  10.3 us (5%)
  matrix products  5.91 us (3%)
  between operations  3.05 us (2%)
    ppermute x11, starting transfers between devices, extended(): after = lax.ppermute(initial, axis, down)  42.7 us
    ppermute x11, waiting for transfers between devices, extended(): before = lax.ppermute(last, axis, up)  40.9 us
    ppermute x11, starting transfers between devices, extended(): before = lax.ppermute(last, axis, up)  32.3 us
    all_to_all x1, blocking collectives, shards(): lax.all_to_all(pieces, 'gz', split_axis=1, concat_axis=1, tiled=True)  10.3 us
    ppermute x11, waiting for transfers between devices, extended(): after = lax.ppermute(initial, axis, down)  9.37 us
    convert_element_type x1, other arithmetic, shards(): level_out.astype(jnp.bfloat16)  9.35 us
    add x1, other arithmetic, shards(): 0.75 * level_set  8.59 us
    add x1, other arithmetic, shards(): section_one = level_set + time_step * section_rate(level_set)  8.38 us
  transfers between devices with their start and end apart: 22, of which 14 were waited for; matrix products, arithmetic and copies ran while one was open for 3% of the time, Pallas kernels for 0%

commit v1 on v0

--- a/solution.py
+++ b/solution.py
@@ -134,7 +134,15 @@
     rows_each = slab_image.shape[1] // group
     columns = slab_image.shape[2]
     pieces = slab_image.reshape(4, group, rows_each, columns)
-    received = lax.all_to_all(pieces, "gz", split_axis=1, concat_axis=1, tiled=True)
+
+    def _end_paths(obj):
+        fresh = lax.axis_size("gz")
+        vec_out = jnp.split(obj, fresh, 1)
+        u_next = jnp.stack(vec_out, 0)
+        plain = lax.all_to_all(u_next, "gz", 0, 0)
+        return jnp.concatenate(plain, 1)
+
+    received = _end_paths(pieces)
     blended = jnp.concatenate(
         [
             jnp.zeros((3, rows_each, columns), jnp.float32),

time: 197 us -> 200 us (1.015)
  local copies, waits for them, and re-layouts: 15.9 us -> 19.3 us
    another operation x1 -> x5, local copies, waits for them, and re-layouts: 0.68 us -> 4.12 us  [_end_paths(): u_next = jnp.stack(vec_out, 0)]
where the time goes in v1:
time: 200 us; the launch traced here: 199 us
  starting transfers between devices  75 us (38%)
  waiting for transfers between devices  50.2 us (25%)
  other arithmetic  35.4 us (18%)
  local copies, waits for them, and re-layouts  19.3 us (10%)
  blocking collectives  10.3 us (5%)
  matrix products  5.92 us (3%)
  between operations  3.13 us (2%)
    ppermute x11, starting transfers between devices, extended(): after = lax.ppermute(initial, axis, down)  42.7 us
    ppermute x11, waiting for transfers between devices, extended(): before = lax.ppermute(last, axis, up)  40.8 us
    ppermute x11, starting transfers between devices, extended(): before = lax.ppermute(last, axis, up)  32.3 us
    all_to_all x1, blocking collectives, _end_paths(): plain = lax.all_to_all(u_next, 'gz', 0, 0)  10.3 us
    ppermute x11, waiting for transfers between devices, extended(): after = lax.ppermute(initial, axis, down)  9.39 us
    convert_element_type x1, other arithmetic, shards(): level_out.astype(jnp.bfloat16)  9.35 us
    add x1, other arithmetic, shards(): 0.75 * level_set  8.59 us
    add x1, other arithmetic, shards(): section_one = level_set + time_step * section_rate(level_set)  8.38 us
  transfers between devices with their start and end apart: 22, of which 14 were waited for; matrix products, arithmetic and copies ran while one was open for 3% of the time, Pallas kernels for 0%

profile of v1, /device:TPU:32, one launch (start us, length us, event | category | flops | bytes accessed | tf_op | source)
XLA Modules:
  0.0 199.3 jit_solution(1236003350197501221)
XLA Ops:
  3.4 13.5 %collective-permute-start.1 = (f32[3,32,128]{2,1,0:T(8,128)S(1)}, f32[3,32,128]{2,1,0:T(8,128)S(1)}, u32[]{:S(2)}, u32[]{:S(2)}) collective-permute-start(f32[3,32,128]{2,1,0:T(8,128)S(1)} %get-tuple-element.59), channel_id=1, source_target_pairs={{16,0},{32,16},{48,32},{64,48},{80,64},{96,80},{112,96},{128,112},... | collective-permute-start | bytes 147464 | tf_op jit(solution)/shard_map/ppermute | solution.py:19
  18.6 4.9 %collective-permute-start.3 = (f32[38,3,128]{2,1,0:T(4,128)S(1)}, f32[38,3,128]{2,1,0:T(4,128)S(1)}, u32[]{:S(2)}, u32[]{:S(2)}) collective-permute-start(f32[38,3,128]{2,1,0:T(4,128)S(1)} %get-tuple-element.51), channel_id=1, source_target_pairs={{4,0},{8,4},{12,8},{0,12},{5,1},{9,5},{13,9},{1,13},{6,2},{10,6},{... | collective-permute-start | bytes 175112 | tf_op jit(solution)/shard_map/ppermute | solution.py:19
  23.6 1.9 collective-permute-start.2
  25.6 5.5 %collective-permute-done.2 = f32[38,3,128]{2,1,0:T(4,128)S(1)} collective-permute-done((f32[38,3,128]{2,1,0:T(4,128)S(1)}, f32[38,3,128]{2,1,0:T(4,128)S(1)}, u32[]{:S(2)}, u32[]{:S(2)}) %collective-permute-start.2) | collective-permute-done | bytes 58400 | tf_op jit(solution)/shard_map/ppermute | solution.py:18
  32.4 2.9 %collective-permute-start.4 = (f32[38,38,3]{1,0,2:T(8,128)}, f32[38,38,3]{1,0,2:T(8,128)S(1)}, u32[]{:S(2)}, u32[]{:S(2)}) collective-permute-start(f32[38,38,3]{1,0,2:T(8,128)} %copy.10), channel_id=1, source_target_pairs={{0,1},{1,2},{2,3},{3,0},{4,5},{5,6},{6,7},{7,4},{8,9},{9,10},{10,1... | collective-permute-start | bytes 51992 | tf_op jit(solution)/shard_map/ppermute | solution.py:18
  35.7 2.9 %collective-permute-start.5 = (f32[38,38,3]{1,0,2:T(8,128)S(1)}, f32[38,38,3]{1,0,2:T(8,128)S(1)}, u32[]{:S(2)}, u32[]{:S(2)}) collective-permute-start(f32[38,38,3]{1,0,2:T(8,128)S(1)} %copy.12), channel_id=1, source_target_pairs={{1,0},{2,1},{3,2},{0,3},{5,4},{6,5},{7,6},{4,7},{9,8},{10,9},{11,1... | collective-permute-start | bytes 51992 | tf_op jit(solution)/shard_map/ppermute | solution.py:19
  39.1 2.7 %collective-permute-done.5 = f32[38,38,3]{1,0,2:T(8,128)S(1)} collective-permute-done((f32[38,38,3]{1,0,2:T(8,128)S(1)}, f32[38,38,3]{1,0,2:T(8,128)S(1)}, u32[]{:S(2)}, u32[]{:S(2)}) %collective-permute-start.5) | collective-permute-done | bytes 17360 | tf_op jit(solution)/shard_map/ppermute | solution.py:19
  43.1 2.0 maximum_maximum_fusion
  45.1 8.4 %fusion.27 = f32[32,32,128]{2,1,0:T(8,128)S(1)} fusion(f32[32,32,128]{2,1,0:T(8,128)S(1)} %copy-done, f32[38,38,131]{2,1,0:T(8,128)S(1)} %get-tuple-element.33, f32[38,38,131]{2,1,0:T(8,128)S(1)} %get-tuple-element.32, f32[38,3,128]{2,1,0:T(4,128)S(1)} %collective-permute-done.3, f32[38,32,128]{2,1,0:T(8,128)S(1)} %get-tuple-element.71, ...), kind=kLoop, calls=%fused_computation.81 | loop fusion | flops 54919168 | bytes 8865792 | tf_op jit(solution)/shard_map/add | solution.py:113
  53.5 7.0 %collective-permute-start.7 = (f32[3,32,128]{2,1,0:T(8,128)S(1)}, f32[3,32,128]{2,1,0:T(8,128)S(1)}, u32[]{:S(2)}, u32[]{:S(2)}) collective-permute-start(f32[3,32,128]{2,1,0:T(8,128)S(1)} %get-tuple-element.55), channel_id=1, source_target_pairs={{16,0},{32,16},{48,32},{64,48},{80,64},{96,80},{112,96},{128,112},... | collective-permute-start | bytes 147464 | tf_op jit(solution)/shard_map/ppermute | solution.py:19
  62.4 9.7 %collective-permute-done.6 = f32[3,32,128]{2,1,0:T(8,128)S(1)} collective-permute-done((f32[3,32,128]{2,1,0:T(8,128)S(1)}, f32[3,32,128]{2,1,0:T(8,128)S(1)}, u32[]{:S(2)}, u32[]{:S(2)}) %collective-permute-start.6) | collective-permute-done | bytes 49184 | tf_op jit(solution)/shard_map/ppermute | solution.py:18
  74.1 3.9 %collective-permute-start.8 = (f32[38,3,128]{2,1,0:T(4,128)S(1)}, f32[38,3,128]{2,1,0:T(4,128)S(1)}, u32[]{:S(2)}, u32[]{:S(2)}) collective-permute-start(f32[38,3,128]{2,1,0:T(4,128)S(1)} %get-tuple-element.48), channel_id=1, source_target_pairs={{0,4},{4,8},{8,12},{12,0},{1,5},{5,9},{9,13},{13,1},{2,6},{6,10},{... | collective-permute-start | bytes 175112 | tf_op jit(solution)/shard_map/ppermute | solution.py:18
  78.4 3.1 %collective-permute-done.8 = f32[38,3,128]{2,1,0:T(4,128)S(1)} collective-permute-done((f32[38,3,128]{2,1,0:T(4,128)S(1)}, f32[38,3,128]{2,1,0:T(4,128)S(1)}, u32[]{:S(2)}, u32[]{:S(2)}) %collective-permute-start.8) | collective-permute-done | bytes 58400 | tf_op jit(solution)/shard_map/ppermute | solution.py:18
  82.3 3.4 %collective-permute-start.10 = (f32[38,38,3]{1,0,2:T(8,128)S(1)}, f32[38,38,3]{1,0,2:T(8,128)S(1)}, u32[]{:S(2)}, u32[]{:S(2)}) collective-permute-start(f32[38,38,3]{1,0,2:T(8,128)S(1)} %copy.14), channel_id=1, source_target_pairs={{0,1},{1,2},{2,3},{3,0},{4,5},{5,6},{6,7},{7,4},{8,9},{9,10},{10,1... | collective-permute-start | bytes 51992 | tf_op jit(solution)/shard_map/ppermute | solution.py:18
  86.1 2.4 %collective-permute-start.11 = (f32[38,38,3]{1,0,2:T(8,128)S(1)}, f32[38,38,3]{1,0,2:T(8,128)S(1)}, u32[]{:S(2)}, u32[]{:S(2)}) collective-permute-start(f32[38,38,3]{1,0,2:T(8,128)S(1)} %copy.16), channel_id=1, source_target_pairs={{1,0},{2,1},{3,2},{0,3},{5,4},{6,5},{7,6},{4,7},{9,8},{10,9},{11,1... | collective-permute-start | bytes 51992 | tf_op jit(solution)/shard_map/ppermute | solution.py:19
  90.0 3.1 %collective-permute-done.11 = f32[38,38,3]{1,0,2:T(8,128)S(1)} collective-permute-done((f32[38,38,3]{1,0,2:T(8,128)S(1)}, f32[38,38,3]{1,0,2:T(8,128)S(1)}, u32[]{:S(2)}, u32[]{:S(2)}) %collective-permute-start.11) | collective-permute-done | bytes 17360 | tf_op jit(solution)/shard_map/ppermute | solution.py:19
  94.4 2.2 %maximum_maximum_fusion.1 = (f32[38,38,131]{2,1,0:T(8,128)S(1)}, f32[38,38,131]{2,1,0:T(8,128)S(1)}) fusion(f32[38,3,128]{2,1,0:T(4,128)S(1)} %collective-permute-done.9, f32[3,32,128]{2,1,0:T(8,128)S(1)} %collective-permute-done.7, f32[32,32,128]{2,1,0:T(8,128)S(1)} %fusion.27, f32[3,32,128]{2,1,0:T(8,128)S(1)} %collective-permute-done.6, ...), kind=kLoop, calls=%fused_computation.2 | loop fusion | flops 1891640 | bytes 2287296 | tf_op jit(solution)/shard_map/concatenate | solution.py:20
  96.6 8.6 %fusion.37 = f32[32,32,128]{2,1,0:T(8,128)S(1)} fusion(f32[32,32,128]{2,1,0:T(8,128)S(1)} %fusion.27, f32[38,38,131]{2,1,0:T(8,128)S(1)} %get-tuple-element.29, f32[38,38,131]{2,1,0:T(8,128)S(1)} %get-tuple-element.28, f32[38,35,128]{2,1,0:T(8,128)S(1)} %get-tuple-element.47, f32[38,35,128]{2,1,0:T(8,128)S(1)} %get-tuple-element.46, ...), kind=kLoop, calls=%fused_computation.91 | loop fusion | flops 55312384 | bytes 8749056 | tf_op jit(solution)/shard_map/add | solution.py:114
  107.1 2.4 %collective-permute-start.12 = (f32[3,32,128]{2,1,0:T(8,128)S(1)}, f32[3,32,128]{2,1,0:T(8,128)S(1)}, u32[]{:S(2)}, u32[]{:S(2)}) collective-permute-start(f32[3,32,128]{2,1,0:T(8,128)S(1)} %get-tuple-element.52), channel_id=1, source_target_pairs={{0,16},{16,32},{32,48},{48,64},{64,80},{80,96},{96,112},{112,128},... | collective-permute-start | bytes 147464 | tf_op jit(solution)/shard_map/ppermute | solution.py:18
  109.5 9.6 %collective-permute-done.12 = f32[3,32,128]{2,1,0:T(8,128)S(1)} collective-permute-done((f32[3,32,128]{2,1,0:T(8,128)S(1)}, f32[3,32,128]{2,1,0:T(8,128)S(1)}, u32[]{:S(2)}, u32[]{:S(2)}) %collective-permute-start.12) | collective-permute-done | bytes 49184 | tf_op jit(solution)/shard_map/ppermute | solution.py:18
  121.1 3.9 %collective-permute-start.14 = (f32[38,3,128]{2,1,0:T(4,128)S(1)}, f32[38,3,128]{2,1,0:T(4,128)S(1)}, u32[]{:S(2)}, u32[]{:S(2)}) collective-permute-start(f32[38,3,128]{2,1,0:T(4,128)S(1)} %get-tuple-element.44), channel_id=1, source_target_pairs={{0,4},{4,8},{8,12},{12,0},{1,5},{5,9},{9,13},{13,1},{2,6},{6,10},{... | collective-permute-start | bytes 175112 | tf_op jit(solution)/shard_map/ppermute | solution.py:18
  125.7 2.9 %collective-permute-done.14 = f32[38,3,128]{2,1,0:T(4,128)S(1)} collective-permute-done((f32[38,3,128]{2,1,0:T(4,128)S(1)}, f32[38,3,128]{2,1,0:T(4,128)S(1)}, u32[]{:S(2)}, u32[]{:S(2)}) %collective-permute-start.14) | collective-permute-done | bytes 58400 | tf_op jit(solution)/shard_map/ppermute | solution.py:18
  129.3 3.9 %collective-permute-start.16 = (f32[38,38,3]{1,0,2:T(8,128)S(1)}, f32[38,38,3]{1,0,2:T(8,128)S(1)}, u32[]{:S(2)}, u32[]{:S(2)}) collective-permute-start(f32[38,38,3]{1,0,2:T(8,128)S(1)} %copy.18), channel_id=1, source_target_pairs={{0,1},{1,2},{2,3},{3,0},{4,5},{5,6},{6,7},{7,4},{8,9},{9,10},{10,1... | collective-permute-start | bytes 51992 | tf_op jit(solution)/shard_map/ppermute | solution.py:18
  133.6 2.1 %collective-permute-start.17 = (f32[38,38,3]{1,0,2:T(8,128)S(1)}, f32[38,38,3]{1,0,2:T(8,128)S(1)}, u32[]{:S(2)}, u32[]{:S(2)}) collective-permute-start(f32[38,38,3]{1,0,2:T(8,128)S(1)} %copy.20), channel_id=1, source_target_pairs={{1,0},{2,1},{3,2},{0,3},{5,4},{6,5},{7,6},{4,7},{9,8},{10,9},{11,1... | collective-permute-start | bytes 51992 | tf_op jit(solution)/shard_map/ppermute | solution.py:19
  137.1 2.6 %collective-permute-done.17 = f32[38,38,3]{1,0,2:T(8,128)S(1)} collective-permute-done((f32[38,38,3]{1,0,2:T(8,128)S(1)}, f32[38,38,3]{1,0,2:T(8,128)S(1)}, u32[]{:S(2)}, u32[]{:S(2)}) %collective-permute-start.17) | collective-permute-done | bytes 17360 | tf_op jit(solution)/shard_map/ppermute | solution.py:19
  141.0 2.2 %maximum_maximum_fusion.2 = (f32[38,38,131]{2,1,0:T(8,128)S(1)}, f32[38,38,131]{2,1,0:T(8,128)S(1)}) fusion(f32[38,3,128]{2,1,0:T(4,128)S(1)} %collective-permute-done.15, f32[3,32,128]{2,1,0:T(8,128)S(1)} %collective-permute-done.13, f32[32,32,128]{2,1,0:T(8,128)S(1)} %fusion.37, f32[3,32,128]{2,1,0:T(8,128)S(1)} %collective-permute-done.12, ...), kind=kLoop, calls=%fused_computation.4 | loop fusion | flops 1891640 | bytes 2287296 | tf_op jit(solution)/shard_map/concatenate | solution.py:20
  143.2 9.4 %fusion.219 = (bf16[32,32,128]{2,1,0:T(8,128)(2,1)S(1)}, f32[32,32,128]{2,1,0:T(8,128)}) fusion(f32[32,32,128]{2,1,0:T(8,128)S(1)} %copy-done, f32[32,32,128]{2,1,0:T(8,128)S(1)} %fusion.37, f32[38,38,131]{2,1,0:T(8,128)S(1)} %get-tuple-element.25, f32[38,38,131]{2,1,0:T(8,128)S(1)} %get-tuple-element.24, bf16[3,32,32,128]{3,2,1,0:T(8,128)(2,1)S(1)} %copy-done.3, ...), kind=kLoop, calls=%fused_computation.363 | loop fusion | flops 55574528 | bytes 9011201 | tf_op jit(solution)/shard_map/convert_element_type | solution.py:121
  154.5 2.4 %collective-permute-start.18 = (bf16[1,32,128]{2,1,0:T(8,128)(2,1)S(1)}, bf16[1,32,128]{2,1,0:T(8,128)(2,1)S(1)}, u32[]{:S(2)}, u32[]{:S(2)}) collective-permute-start(bf16[1,32,128]{2,1,0:T(8,128)(2,1)S(1)} %get-tuple-element.63), channel_id=1, source_target_pairs={{0,16},{16,32},{32,48},{48,64},{64,80},{80,96},{96,112},{112,128},... | collective-permute-start | bytes 24584 | tf_op jit(solution)/shard_map/ppermute | solution.py:18
  156.9 8.6 %collective-permute-done.18 = bf16[1,32,128]{2,1,0:T(8,128)(2,1)S(1)} collective-permute-done((bf16[1,32,128]{2,1,0:T(8,128)(2,1)S(1)}, bf16[1,32,128]{2,1,0:T(8,128)(2,1)S(1)}, u32[]{:S(2)}, u32[]{:S(2)}) %collective-permute-start.18) | collective-permute-done | bytes 8224 | tf_op jit(solution)/shard_map/ppermute | solution.py:18
  165.5 2.2 %collective-permute-start.21 = (bf16[34,1,128]{2,1,0:T(2,128)(2,1)S(1)}, bf16[34,1,128]{2,1,0:T(2,128)(2,1)S(1)}, u32[]{:S(2)}, u32[]{:S(2)}) collective-permute-start(bf16[34,1,128]{2,1,0:T(2,128)(2,1)S(1)} %get-tuple-element.62), channel_id=1, source_target_pairs={{4,0},{8,4},{12,8},{0,12},{5,1},{9,5},{13,9},{1,13},{6,2},{10,6},{... | collective-permute-start | bytes 26120 | tf_op jit(solution)/shard_map/ppermute | solution.py:19
  167.7 3.6 %collective-permute-start.20 = (bf16[34,1,128]{2,1,0:T(2,128)(2,1)S(1)}, bf16[34,1,128]{2,1,0:T(2,128)(2,1)S(1)}, u32[]{:S(2)}, u32[]{:S(2)}) collective-permute-start(bf16[34,1,128]{2,1,0:T(2,128)(2,1)S(1)} %get-tuple-element.61), channel_id=1, source_target_pairs={{0,4},{4,8},{8,12},{12,0},{1,5},{5,9},{9,13},{13,1},{2,6},{6,10},{... | collective-permute-start | bytes 26120 | tf_op jit(solution)/shard_map/ppermute | solution.py:18
  185.6 10.3 %all_to_all.5 = f32[4,1,4096]{2,1,0:T(1,128)S(1)} all-to-all(f32[4,1,4096]{2,1,0:T(1,128)S(1)} %reshape.87), channel_id=1, replica_groups=mesh['gx'=32,'gy'=4,'gz'=4] {'gz'}, dimensions={0} | all-to-all | bytes 131072 | tf_op jit(solution)/shard_map/all_to_all | solution.py:142
  (97 shorter events, 42.0 us)
Async XLA Ops:
  1.5 15.4 %collective-permute-start = (f32[3,32,128]{2,1,0:T(8,128)S(1)}, f32[3,32,128]{2,1,0:T(8,128)S(1)}, u32[]{:S(2)}, u32[]{:S(2)}) collective-permute-start(f32[3,32,128]{2,1,0:T(8,128)S(1)} %get-tuple-element.60), channel_id=1, source_target_pairs={{0,16},{16,32},{32,48},{48,64},{64,80},{80,96},{96,112},{112,128},... | collective-permute-start | bytes 147464 | tf_op jit(solution)/shard_map/ppermute | solution.py:18
  3.4 15.2 %collective-permute-start.1 = (f32[3,32,128]{2,1,0:T(8,128)S(1)}, f32[3,32,128]{2,1,0:T(8,128)S(1)}, u32[]{:S(2)}, u32[]{:S(2)}) collective-permute-start(f32[3,32,128]{2,1,0:T(8,128)S(1)} %get-tuple-element.59), channel_id=1, source_target_pairs={{16,0},{32,16},{48,32},{64,48},{80,64},{96,80},{112,96},{128,112},... | collective-permute-start | bytes 147464 | tf_op jit(solution)/shard_map/ppermute | solution.py:19
  18.6 6.9 %collective-permute-start.3 = (f32[38,3,128]{2,1,0:T(4,128)S(1)}, f32[38,3,128]{2,1,0:T(4,128)S(1)}, u32[]{:S(2)}, u32[]{:S(2)}) collective-permute-start(f32[38,3,128]{2,1,0:T(4,128)S(1)} %get-tuple-element.51), channel_id=1, source_target_pairs={{4,0},{8,4},{12,8},{0,12},{5,1},{9,5},{13,9},{1,13},{6,2},{10,6},{... | collective-permute-start | bytes 175112 | tf_op jit(solution)/shard_map/ppermute | solution.py:19
  23.6 7.5 %collective-permute-start.2 = (f32[38,3,128]{2,1,0:T(4,128)S(1)}, f32[38,3,128]{2,1,0:T(4,128)S(1)}, u32[]{:S(2)}, u32[]{:S(2)}) collective-permute-start(f32[38,3,128]{2,1,0:T(4,128)S(1)} %get-tuple-element.50), channel_id=1, source_target_pairs={{0,4},{4,8},{8,12},{12,0},{1,5},{5,9},{9,13},{13,1},{2,6},{6,10},{... | collective-permute-start | bytes 175112 | tf_op jit(solution)/shard_map/ppermute | solution.py:18
  32.4 6.3 %collective-permute-start.4 = (f32[38,38,3]{1,0,2:T(8,128)}, f32[38,38,3]{1,0,2:T(8,128)S(1)}, u32[]{:S(2)}, u32[]{:S(2)}) collective-permute-start(f32[38,38,3]{1,0,2:T(8,128)} %copy.10), channel_id=1, source_target_pairs={{0,1},{1,2},{2,3},{3,0},{4,5},{5,6},{6,7},{7,4},{8,9},{9,10},{10,1... | collective-permute-start | bytes 51992 | tf_op jit(solution)/shard_map/ppermute | solution.py:18
  35.7 6.1 %collective-permute-start.5 = (f32[38,38,3]{1,0,2:T(8,128)S(1)}, f32[38,38,3]{1,0,2:T(8,128)S(1)}, u32[]{:S(2)}, u32[]{:S(2)}) collective-permute-start(f32[38,38,3]{1,0,2:T(8,128)S(1)} %copy.12), channel_id=1, source_target_pairs={{1,0},{2,1},{3,2},{0,3},{5,4},{6,5},{7,6},{4,7},{9,8},{10,9},{11,1... | collective-permute-start | bytes 51992 | tf_op jit(solution)/shard_map/ppermute | solution.py:19
  43.1 2.0 copy-start
  43.1 2.0 copy-start.1
  53.5 8.9 %collective-permute-start.7 = (f32[3,32,128]{2,1,0:T(8,128)S(1)}, f32[3,32,128]{2,1,0:T(8,128)S(1)}, u32[]{:S(2)}, u32[]{:S(2)}) collective-permute-start(f32[3,32,128]{2,1,0:T(8,128)S(1)} %get-tuple-element.55), channel_id=1, source_target_pairs={{16,0},{32,16},{48,32},{64,48},{80,64},{96,80},{112,96},{128,112},... | collective-permute-start | bytes 147464 | tf_op jit(solution)/shard_map/ppermute | solution.py:19
  60.5 11.6 %collective-permute-start.6 = (f32[3,32,128]{2,1,0:T(8,128)S(1)}, f32[3,32,128]{2,1,0:T(8,128)S(1)}, u32[]{:S(2)}, u32[]{:S(2)}) collective-permute-start(f32[3,32,128]{2,1,0:T(8,128)S(1)} %get-tuple-element.54), channel_id=1, source_target_pairs={{0,16},{16,32},{32,48},{48,64},{64,80},{80,96},{96,112},{112,128},... | collective-permute-start | bytes 147464 | tf_op jit(solution)/shard_map/ppermute | solution.py:18
  72.2 6.3 %collective-permute-start.9 = (f32[38,3,128]{2,1,0:T(4,128)S(1)}, f32[38,3,128]{2,1,0:T(4,128)S(1)}, u32[]{:S(2)}, u32[]{:S(2)}) collective-permute-start(f32[38,3,128]{2,1,0:T(4,128)S(1)} %get-tuple-element.49), channel_id=1, source_target_pairs={{4,0},{8,4},{12,8},{0,12},{5,1},{9,5},{13,9},{1,13},{6,2},{10,6},{... | collective-permute-start | bytes 175112 | tf_op jit(solution)/shard_map/ppermute | solution.py:19
  74.1 7.5 %collective-permute-start.8 = (f32[38,3,128]{2,1,0:T(4,128)S(1)}, f32[38,3,128]{2,1,0:T(4,128)S(1)}, u32[]{:S(2)}, u32[]{:S(2)}) collective-permute-start(f32[38,3,128]{2,1,0:T(4,128)S(1)} %get-tuple-element.48), channel_id=1, source_target_pairs={{0,4},{4,8},{8,12},{12,0},{1,5},{5,9},{9,13},{13,1},{2,6},{6,10},{... | collective-permute-start | bytes 175112 | tf_op jit(solution)/shard_map/ppermute | solution.py:18
  82.3 6.4 %collective-permute-start.10 = (f32[38,38,3]{1,0,2:T(8,128)S(1)}, f32[38,38,3]{1,0,2:T(8,128)S(1)}, u32[]{:S(2)}, u32[]{:S(2)}) collective-permute-start(f32[38,38,3]{1,0,2:T(8,128)S(1)} %copy.14), channel_id=1, source_target_pairs={{0,1},{1,2},{2,3},{3,0},{4,5},{5,6},{6,7},{7,4},{8,9},{9,10},{10,1... | collective-permute-start | bytes 51992 | tf_op jit(solution)/shard_map/ppermute | solution.py:18
  86.1 7.0 %collective-permute-start.11 = (f32[38,38,3]{1,0,2:T(8,128)S(1)}, f32[38,38,3]{1,0,2:T(8,128)S(1)}, u32[]{:S(2)}, u32[]{:S(2)}) collective-permute-start(f32[38,38,3]{1,0,2:T(8,128)S(1)} %copy.16), channel_id=1, source_target_pairs={{1,0},{2,1},{3,2},{0,3},{5,4},{6,5},{7,6},{4,7},{9,8},{10,9},{11,1... | collective-permute-start | bytes 51992 | tf_op jit(solution)/shard_map/ppermute | solution.py:19
  94.4 2.2 %copy-start.2 = (bf16[3,32,32,128]{3,2,1,0:T(8,128)(2,1)S(1)}, bf16[3,32,32,128]{3,2,1,0:T(8,128)(2,1)}, u32[]{:S(2)}) copy-start(bf16[3,32,32,128]{3,2,1,0:T(8,128)(2,1)} %param.5) | copy-start | bytes 2359300
  105.2 4.3 %collective-permute-start.13 = (f32[3,32,128]{2,1,0:T(8,128)S(1)}, f32[3,32,128]{2,1,0:T(8,128)S(1)}, u32[]{:S(2)}, u32[]{:S(2)}) collective-permute-start(f32[3,32,128]{2,1,0:T(8,128)S(1)} %get-tuple-element.53), channel_id=1, source_target_pairs={{16,0},{32,16},{48,32},{64,48},{80,64},{96,80},{112,96},{128,112},... | collective-permute-start | bytes 147464 | tf_op jit(solution)/shard_map/ppermute | solution.py:19
  107.1 12.0 %collective-permute-start.12 = (f32[3,32,128]{2,1,0:T(8,128)S(1)}, f32[3,32,128]{2,1,0:T(8,128)S(1)}, u32[]{:S(2)}, u32[]{:S(2)}) collective-permute-start(f32[3,32,128]{2,1,0:T(8,128)S(1)} %get-tuple-element.52), channel_id=1, source_target_pairs={{0,16},{16,32},{32,48},{48,64},{64,80},{80,96},{96,112},{112,128},... | collective-permute-start | bytes 147464 | tf_op jit(solution)/shard_map/ppermute | solution.py:18
  119.1 6.5 %collective-permute-start.15 = (f32[38,3,128]{2,1,0:T(4,128)S(1)}, f32[38,3,128]{2,1,0:T(4,128)S(1)}, u32[]{:S(2)}, u32[]{:S(2)}) collective-permute-start(f32[38,3,128]{2,1,0:T(4,128)S(1)} %get-tuple-element.45), channel_id=1, source_target_pairs={{4,0},{8,4},{12,8},{0,12},{5,1},{9,5},{13,9},{1,13},{6,2},{10,6},{... | collective-permute-start | bytes 175112 | tf_op jit(solution)/shard_map/ppermute | solution.py:19
  121.1 7.5 %collective-permute-start.14 = (f32[38,3,128]{2,1,0:T(4,128)S(1)}, f32[38,3,128]{2,1,0:T(4,128)S(1)}, u32[]{:S(2)}, u32[]{:S(2)}) collective-permute-start(f32[38,3,128]{2,1,0:T(4,128)S(1)} %get-tuple-element.44), channel_id=1, source_target_pairs={{0,4},{4,8},{8,12},{12,0},{1,5},{5,9},{9,13},{13,1},{2,6},{6,10},{... | collective-permute-start | bytes 175112 | tf_op jit(solution)/shard_map/ppermute | solution.py:18
  129.3 6.5 %collective-permute-start.16 = (f32[38,38,3]{1,0,2:T(8,128)S(1)}, f32[38,38,3]{1,0,2:T(8,128)S(1)}, u32[]{:S(2)}, u32[]{:S(2)}) collective-permute-start(f32[38,38,3]{1,0,2:T(8,128)S(1)} %copy.18), channel_id=1, source_target_pairs={{0,1},{1,2},{2,3},{3,0},{4,5},{5,6},{6,7},{7,4},{8,9},{9,10},{10,1... | collective-permute-start | bytes 51992 | tf_op jit(solution)/shard_map/ppermute | solution.py:18
  133.6 6.1 %collective-permute-start.17 = (f32[38,38,3]{1,0,2:T(8,128)S(1)}, f32[38,38,3]{1,0,2:T(8,128)S(1)}, u32[]{:S(2)}, u32[]{:S(2)}) collective-permute-start(f32[38,38,3]{1,0,2:T(8,128)S(1)} %copy.20), channel_id=1, source_target_pairs={{1,0},{2,1},{3,2},{0,3},{5,4},{6,5},{7,6},{4,7},{9,8},{10,9},{11,1... | collective-permute-start | bytes 51992 | tf_op jit(solution)/shard_map/ppermute | solution.py:19
  141.0 2.2 %copy-start.3 = (bf16[3,32,32,128]{3,2,1,0:T(8,128)(2,1)S(1)}, bf16[3,32,32,128]{3,2,1,0:T(8,128)(2,1)}, u32[]{:S(2)}) copy-start(bf16[3,32,32,128]{3,2,1,0:T(8,128)(2,1)} %param.5) | copy-start | bytes 2359300
  143.2 28.2 %copy-start.4 = (s32[4]{0:T(128)S(1)}, s32[4]{0:T(128)}, u32[]{:S(2)}) copy-start(s32[4]{0:T(128)} %param.7) | copy-start | bytes 52
  152.6 4.3 %collective-permute-start.19 = (bf16[1,32,128]{2,1,0:T(8,128)(2,1)S(1)}, bf16[1,32,128]{2,1,0:T(8,128)(2,1)S(1)}, u32[]{:S(2)}, u32[]{:S(2)}) collective-permute-start(bf16[1,32,128]{2,1,0:T(8,128)(2,1)S(1)} %get-tuple-element.64), channel_id=1, source_target_pairs={{16,0},{32,16},{48,32},{64,48},{80,64},{96,80},{112,96},{128,112},... | collective-permute-start | bytes 24584 | tf_op jit(solution)/shard_map/ppermute | solution.py:19
  154.5 11.0 %collective-permute-start.18 = (bf16[1,32,128]{2,1,0:T(8,128)(2,1)S(1)}, bf16[1,32,128]{2,1,0:T(8,128)(2,1)S(1)}, u32[]{:S(2)}, u32[]{:S(2)}) collective-permute-start(bf16[1,32,128]{2,1,0:T(8,128)(2,1)S(1)} %get-tuple-element.63), channel_id=1, source_target_pairs={{0,16},{16,32},{32,48},{48,64},{64,80},{80,96},{96,112},{112,128},... | collective-permute-start | bytes 24584 | tf_op jit(solution)/shard_map/ppermute | solution.py:18
  165.5 7.7 %collective-permute-start.21 = (bf16[34,1,128]{2,1,0:T(2,128)(2,1)S(1)}, bf16[34,1,128]{2,1,0:T(2,128)(2,1)S(1)}, u32[]{:S(2)}, u32[]{:S(2)}) collective-permute-start(bf16[34,1,128]{2,1,0:T(2,128)(2,1)S(1)} %get-tuple-element.62), channel_id=1, source_target_pairs={{4,0},{8,4},{12,8},{0,12},{5,1},{9,5},{13,9},{1,13},{6,2},{10,6},{... | collective-permute-start | bytes 26120 | tf_op jit(solution)/shard_map/ppermute | solution.py:19
  167.7 6.9 %collective-permute-start.20 = (bf16[34,1,128]{2,1,0:T(2,128)(2,1)S(1)}, bf16[34,1,128]{2,1,0:T(2,128)(2,1)S(1)}, u32[]{:S(2)}, u32[]{:S(2)}) collective-permute-start(bf16[34,1,128]{2,1,0:T(2,128)(2,1)S(1)} %get-tuple-element.61), channel_id=1, source_target_pairs={{0,4},{4,8},{8,12},{12,0},{1,5},{5,9},{9,13},{13,1},{2,6},{6,10},{... | collective-permute-start | bytes 26120 | tf_op jit(solution)/shard_map/ppermute | solution.py:18
